TPU v7x, 256 devices: a whole 4x4x8 slice. The times are simulated.
256 devices in a mesh: traj: 64 (over z, y, core), mstate: 4 (over x).
Axes of the slice: x: 4, y: 4, z: 8, core: 2. Of those that a mesh axis runs over, the one named last changes fastest.
Arguments:
- bias: float32 [32, 2097152], P(None, ('traj', 'mstate')), may hold values from -206 to 206
- labels: int32 [2097152], P(('traj', 'mstate')), may hold values from 0 to 4095, as said below
- therm_index: int32 [2097152], P(('traj', 'mstate')), may hold values from 0 to 31
- counts: int32 [32, 4096, 4096], P(None, 'traj', 'mstate'), may hold values from 0 to 4, as said below
- free_start: float32 [32, 4096], replicated, may hold values from -6 to 6
- mult_start: float32 [32, 4096], replicated, may hold values from -6 to 6
Outputs:
- free_energy: float32 [32, 4096], P(None, 'mstate')
- log_mult: float32 [32, 4096], P(None, 'mstate')
Inputs may be any that keep to these rules, and one draw needn't show every extreme that they name: `labels`: every Markov state is the label of at least one frame. `counts`: most entries are zero.
All inputs are finite; a program needn't handle non-finite values.
Results may differ from a plain program's by a relative error of at most 0.0001.
Values sent between devices are 32-bit elements; how exact they have to be, the bound alone decides.
No kernel may reach another device: no remote copies, remote signals or barrier semaphores. Data moves between devices by JAX's collectives and lax.ppermute only.
A program may use at most 64 MiB of HBM per device.

v0:
```python
import jax
import jax.numpy as jnp
from jax import lax
from jax.sharding import PartitionSpec as P

ITERS = 2


def per_device(bias, labels, therm_index, counts, free_start, mult_start):
    states_k = bias.shape[0]
    width = free_start.shape[1]
    col_count = counts.shape[1]
    row_count = counts.shape[2]
    col_start = lax.axis_index("traj") * col_count
    row_start = lax.axis_index("mstate") * row_count
    states = jax.nn.one_hot(therm_index, states_k, dtype=jnp.float32)
    local_visits = jax.ops.segment_sum(states, labels, num_segments=width).T
    visits = lax.psum(local_visits, ("traj", "mstate"))
    counts_real = counts.astype(jnp.float32)
    free, mult = (free_start, mult_start)
    for step in range(ITERS):
        free_cols = lax.dynamic_slice_in_dim(free, col_start, col_count, 1)
        mult_cols = lax.dynamic_slice_in_dim(mult, col_start, col_count, 1)
        free_rows = lax.dynamic_slice_in_dim(free, row_start, row_count, 1)
        mult_rows = lax.dynamic_slice_in_dim(mult, row_start, row_count, 1)
        weight = jax.nn.sigmoid(
            mult_rows[:, None, :]
            + free_cols[:, :, None]
            - mult_cols[:, :, None]
            - free_rows[:, None, :]
        )
        partial_rows = jnp.sum(counts_real * weight, axis=1)
        row_total = lax.psum(partial_rows, "traj")
        mult = lax.all_gather(jnp.log(0.5 + row_total), "mstate", axis=1, tiled=True)
        level = jnp.log(jnp.exp(mult) + visits) + free
        scores = jnp.take(level, labels, axis=1) - bias
        top = jnp.max(scores, axis=0)
        logl = top + jnp.log(jnp.sum(jnp.exp(scores - top[None, :]), axis=0))
        term = -bias - logl[None, :]
        shift = lax.pmax(jnp.max(term, axis=1), ("traj", "mstate"))
        weights = jnp.exp(term - shift[:, None])
        local_total = jax.ops.segment_sum(weights.T, labels, num_segments=width).T
        total = lax.psum(local_total, ("traj", "mstate"))
        free = -(shift[:, None] + jnp.log(total))
    free_out = lax.dynamic_slice_in_dim(free, row_start, row_count, 1)
    mult_out = lax.dynamic_slice_in_dim(mult, row_start, row_count, 1)
    return (free_out, mult_out)


def solution(mesh):
    placed = (
        P(None, ("traj", "mstate")),
        P(("traj", "mstate")),
        P(("traj", "mstate")),
        P(None, "traj", "mstate"),
        P(),
        P(),
    )
    return jax.shard_map(
        per_device,
        mesh=mesh,
        in_specs=placed,
        out_specs=(P(None, "mstate"), P(None, "mstate")),
        check_vma=False,
    )
```

profile of v0, /device:TPU:2, one launch (start us, length us, event | category | flops | bytes accessed | tf_op | source)
XLA Modules:
  0.0 1501.2 jit_solution(12562265268010864750)
XLA Ops:
  9.1 6.6 multiply_reduce_fusion.1
  15.8 48.6 %scatter_custom_fusion = f32[4096,32]{1,0:T(8,128)S(1)} fusion(s32[8192]{0:T(1024)S(1)} %copy-done.10, s32[8192]{0:T(1024)S(1)} %copy-done.11, f32[]{:T(128)} %constant.11.clone.1), kind=kCustom, calls=%fused_computation.11 | custom fusion | flops 786432 | bytes 557060 | tf_op jit(solution)/shard_map/scatter-add | solution.py:17
  65.9 2.6 copy.44
  68.5 125.1 %all-reduce.6.cloned.1.call-done = f32[32,1024]{1,0:T(8,128)} async-done(((f32[32,1024]{1,0:T(8,128)}), f32[32,1024]{1,0:T(8,128)}) %all-reduce.6.cloned.1.call-update) | async-done | bytes 131088 | tf_op jit(solution)/shard_map/psum | solution.py:33
  194.5 13.4 all_gather.6
  208.0 245.2 %all-reduce.8.cloned.1.call-done = f32[32,4096]{1,0:T(8,128)} async-done(((f32[32,4096]{1,0:T(8,128)}), f32[32,4096]{1,0:T(8,128)}) %all-reduce.8.cloned.1.call-update) | async-done | bytes 524304 | tf_op jit(solution)/shard_map/psum | solution.py:18
  453.2 2.0 log_add_fusion.1
  456.8 27.7 %gather_fusion = f32[8192,32]{1,0:T(8,128)} fusion(f32[32,4096]{0,1:T(8,128)S(1)} %copy.43, s32[8192]{0:T(1024)S(1)} %fusion.12), kind=kCustom, calls=%fused_computation.clone | custom fusion | bytes 2129920 | tf_op jit(solution)/shard_map/jit(_take)/gather | solution.py:36
  484.5 6.5 fusion.8
  491.1 4.0 exponential_reduce_fusion.1
  495.4 75.6 %pmax.14 = f32[32]{0:T(128)S(1)} all-reduce(f32[32]{0:T(128)S(1)} %subtract_reduce_fusion.1), channel_id=1, replica_groups=mesh['traj'=64,'mstate'=4] {'traj','mstate'}, use_global_device_ids=true, to_apply=%region_7.9 | all-reduce | flops 32 | bytes 256 | tf_op jit(solution)/shard_map/pmax | solution.py:40
  571.2 2.7 copy.45
  573.9 44.8 %scatter_custom_fusion.1 = f32[4096,32]{1,0:T(8,128)S(1)} fusion(s32[8192]{0:T(1024)S(1)} %copy-done.10, f32[8192,32]{1,0:T(8,128)} %copy.45, f32[]{:T(128)} %constant.11.clone.1), kind=kCustom, calls=%fused_computation.19 | custom fusion | flops 262144 | bytes 524800 | tf_op jit(solution)/shard_map/scatter-add | solution.py:42
  622.1 250.2 %all-reduce.10.cloned.1.call-done = f32[32,4096]{1,0:T(8,128)} async-done(((f32[32,4096]{1,0:T(8,128)}), f32[32,4096]{1,0:T(8,128)}) %all-reduce.10.cloned.1.call-update) | async-done | bytes 524304 | tf_op jit(solution)/shard_map/psum | solution.py:43
  873.6 6.7 multiply_reduce_fusion
  880.4 173.8 %all-reduce.12.cloned.1.call-done = f32[32,1024]{1,0:T(8,128)} async-done(((f32[32,1024]{1,0:T(8,128)}), f32[32,1024]{1,0:T(8,128)}) %all-reduce.12.cloned.1.call-update) | async-done | bytes 131088 | tf_op jit(solution)/shard_map/psum | solution.py:33
  1055.1 13.4 all_gather.7
  1072.1 27.7 %gather_fusion.1 = f32[8192,32]{1,0:T(8,128)} fusion(f32[32,4096]{0,1:T(8,128)S(1)} %copy.47, s32[8192]{0:T(1024)S(1)} %fusion.12), kind=kCustom, calls=%fused_computation.1.clone | custom fusion | bytes 2129920 | tf_op jit(solution)/shard_map/jit(_take)/gather | solution.py:36
  1099.8 6.5 fusion.9
  1106.4 4.0 exponential_reduce_fusion
  1110.6 73.3 %pmax.15 = f32[32]{0:T(128)S(1)} all-reduce(f32[32]{0:T(128)S(1)} %subtract_reduce_fusion), channel_id=1, replica_groups=mesh['traj'=64,'mstate'=4] {'traj','mstate'}, use_global_device_ids=true, to_apply=%region_15.17 | all-reduce | flops 32 | bytes 256 | tf_op jit(solution)/shard_map/pmax | solution.py:40
  1184.2 2.6 copy.49
  1186.8 45.7 %scatter_custom_fusion.2 = f32[4096,32]{1,0:T(8,128)} fusion(s32[8192]{0:T(1024)S(1)} %copy-done.10, f32[8192,32]{1,0:T(8,128)} %copy.49, f32[]{:T(128)} %constant.11.clone.1), kind=kCustom, calls=%fused_computation.17 | custom fusion | flops 262144 | bytes 524800 | tf_op jit(solution)/shard_map/scatter-add | solution.py:42
  1234.1 258.6 %all-reduce.14.cloned.1.call-done = f32[32,4096]{0,1:T(8,128)} async-done(((f32[32,4096]{0,1:T(8,128)}), f32[32,4096]{0,1:T(8,128)}) %all-reduce.14.cloned.1.call-update) | async-done | bytes 524304 | tf_op jit(solution)/shard_map/psum | solution.py:43
  (59 shorter events, 19.5 us)
Async XLA Ops:
  7.2 186.5 %all-reduce.6.cloned.1.call-start = ((), (), s32[]{:S(2)}) async-start(), calls=%async_computation | async-start | bytes 262144 | tf_op jit(solution)/shard_map/psum | solution.py:33
  9.0 6.7 copy-start.10
  9.0 6.7 copy-start.11
  15.7 50.2 %copy-start.2 = (f32[32,8192]{1,0:T(8,128)S(1)}, f32[32,8192]{1,0:T(8,128)}, u32[]{:S(2)}) copy-start(f32[32,8192]{1,0:T(8,128)} %param.8) | copy-start | bytes 3145732
  15.7 437.5 %all-reduce.8.cloned.1.call-start = ((), (), s32[]{:S(2)}) async-start(), calls=%async_computation.1 | async-start | bytes 1048576 | tf_op jit(solution)/shard_map/psum | solution.py:18
  65.8 387.4 %copy-start.9 = (f32[32,4096]{1,0:T(8,128)S(1)}, f32[32,4096]{1,0:T(8,128)}, u32[]{:S(2)}) copy-start(f32[32,4096]{1,0:T(8,128)} %param.12) | copy-start | bytes 1572868
  65.8 806.5 %all-reduce.10.cloned.1.call-start = ((), (), s32[]{:S(2)}) async-start(), calls=%async_computation.2 | async-start | bytes 1048576 | tf_op jit(solution)/shard_map/psum | solution.py:43
  208.0 245.2 %copy-start.5 = (f32[32,4096]{1,0:T(8,128)}, f32[32,4096]{1,0:T(8,128)S(1)}, u32[]{:S(2)}) copy-start(f32[32,4096]{1,0:T(8,128)S(1)} %all_gather.6) | copy-start | bytes 1572868
  484.5 6.5 copy-start
  484.5 6.5 copy-start.4
  620.1 434.0 %all-reduce.12.cloned.1.call-start = ((), (), s32[]{:S(2)}) async-start(), calls=%async_computation.3 | async-start | bytes 262144 | tf_op jit(solution)/shard_map/psum | solution.py:33
  873.5 195.9 %copy-start.7 = (f32[32,4096]{1,0:T(8,128)S(1)}, f32[32,4096]{1,0:T(8,128)}, u32[]{:S(2)}) copy-start(f32[32,4096]{1,0:T(8,128)} %all-reduce.10.cloned.1.call-done) | copy-start | bytes 1572868
  873.5 195.8 %copy-start.8 = (f32[32,4096]{1,0:T(8,128)S(1)}, f32[32,4096]{1,0:T(8,128)}, u32[]{:S(2)}) copy-start(f32[32,4096]{1,0:T(8,128)} %all-reduce.8.cloned.1.call-done) | copy-start | bytes 1572868
  880.3 612.4 %all-reduce.14.cloned.1.call-start = ((), (), s32[]{:S(2)}) async-start(), calls=%async_computation.4 | async-start | bytes 4194304 | tf_op jit(solution)/shard_map/psum | solution.py:43
  1068.5 0.9 copy-start.6
  1099.8 6.5 copy-start.1
  1099.8 6.5 copy-start.3
Sparse Core Ops, SparseCore 0:
  15.8 177.7 all-reduce.5
  199.1 254.0 all-reduce.7
  620.2 251.9 all-reduce.9
  880.4 173.6 all-reduce.11
  1232.7 260.0 all-reduce.13
where the time goes:
time: 1500 us
  waiting for transfers between devices  1050 us (70%)
  other arithmetic  182 us (12%)
  blocking collectives  176 us (12%)
  local copies, waits for them, and re-layouts  76.4 us (5%)
    psum x2, waiting for transfers between devices, per_device(): total = lax.psum(local_total, ('traj', 'mstate'))  509 us
    psum x2, waiting for transfers between devices, per_device(): row_total = lax.psum(partial_rows, 'traj')  299 us
    psum x1, waiting for transfers between devices, per_device(): visits = lax.psum(local_visits, ('traj', 'mstate'))  245 us
    pmax x2, blocking collectives, per_device(): shift = lax.pmax(jnp.max(term, axis=1), ('traj', 'mstate'))  149 us
    scatter-add x2, other arithmetic, per_device(): local_total = jax.ops.segment_sum(weights.T, labels, num_segments=width).T  90.5 us
    gather x2, local copies, waits for them, and re-layouts, per_device(): scores = jnp.take(level, labels, axis=1) - bias  55.5 us
    scatter-add x1, other arithmetic, per_device(): local_visits = jax.ops.segment_sum(states, labels, num_segments=width).T  48.6 us
  transfers between devices with their start and end apart: 5, of which 5 were waited for; matrix products, arithmetic and copies ran while one was open for 4% of the time, Pallas kernels for 0%

commit v1 on v0

--- a/solution.py
+++ b/solution.py
@@ -30,7 +30,7 @@
             - free_rows[:, None, :]
         )
         partial_rows = jnp.sum(counts_real * weight, axis=1)
-        row_total = lax.psum(partial_rows, "traj")
+        row_total = jnp.sum(lax.all_gather(partial_rows, "traj"), axis=0)
         mult = lax.all_gather(jnp.log(0.5 + row_total), "mstate", axis=1, tiled=True)
         level = jnp.log(jnp.exp(mult) + visits) + free
         scores = jnp.take(level, labels, axis=1) - bias

time: 1500 us -> 1290 us (0.86)
  waiting for transfers between devices: 1050 us -> 834 us
    psum x2 -> x0, waiting for transfers between devices: 299 us -> none  [per_device(): row_total = lax.psum(partial_rows, 'traj')]
    all_gather x0 -> x2, waiting for transfers between devices: none -> 115 us  [per_device(): row_total = jnp.sum(lax.all_gather(partial_rows, 'traj'), axis=0)]
    psum x1, waiting for transfers between devices: 245 us -> 209 us  [per_device(): visits = lax.psum(local_visits, ('traj', 'mstate'))]
  transfers between devices with their start and end apart: 5 -> 5, of which waited for: 5 -> 5; matrix products, arithmetic and copies ran while one was open for 4% -> 5% of each run, Pallas kernels for 0% -> 0%
where the time goes in v1:
time: 1290 us
  waiting for transfers between devices  834 us (65%)
  other arithmetic  188 us (15%)
  blocking collectives  174 us (13%)
  local copies, waits for them, and re-layouts  76.3 us (6%)
  between operations  15.9 us (1%)
    psum x2, waiting for transfers between devices, per_device(): total = lax.psum(local_total, ('traj', 'mstate'))  509 us
    psum x1, waiting for transfers between devices, per_device(): visits = lax.psum(local_visits, ('traj', 'mstate'))  209 us
    pmax x2, blocking collectives, per_device(): shift = lax.pmax(jnp.max(term, axis=1), ('traj', 'mstate'))  148 us
    all_gather x2, waiting for transfers between devices, per_device(): row_total = jnp.sum(lax.all_gather(partial_rows, 'traj'), axis=0)  115 us
    scatter-add x2, other arithmetic, per_device(): local_total = jax.ops.segment_sum(weights.T, labels, num_segments=width).T  90.5 us
    gather x2, local copies, waits for them, and re-layouts, per_device(): scores = jnp.take(level, labels, axis=1) - bias  55.4 us
    scatter-add x1, other arithmetic, per_device(): local_visits = jax.ops.segment_sum(states, labels, num_segments=width).T  48.6 us
    all_gather x2, blocking collectives, per_device(): lax.all_gather(jnp.log(0.5 + row_total), 'mstate', axis=1, tiled=True)  26.4 us
  transfers between devices with their start and end apart: 5, of which 5 were waited for; matrix products, arithmetic and copies ran while one was open for 5% of the time, Pallas kernels for 0%

profile of v1, /device:TPU:2, one launch (start us, length us, event | category | flops | bytes accessed | tf_op | source)
XLA Modules:
  0.0 1288.3 jit_solution(11508771814225955957)
XLA Ops:
  9.9 6.6 multiply_reduce_fusion.1
  16.6 48.6 %scatter_custom_fusion = f32[4096,32]{1,0:T(8,128)S(1)} fusion(s32[8192]{0:T(1024)S(1)} %copy-done.10, s32[8192]{0:T(1024)S(1)} %copy-done.11, f32[]{:T(128)} %constant.11.clone.1), kind=kCustom, calls=%fused_computation.11 | custom fusion | flops 786432 | bytes 557060 | tf_op jit(solution)/shard_map/scatter-add | solution.py:17
  66.8 2.7 copy.44
  69.5 33.3 %all-gather.5.cloned.1.call-done = f32[2048,1024]{1,0:T(8,128)} async-done(((f32[32,1024]{1,0:T(8,128)}), f32[2048,1024]{1,0:T(8,128)}) %all-gather.5.cloned.1.call-update) | async-done | bytes 8388624 | tf_op jit(solution)/shard_map/all_gather | solution.py:33
  102.8 4.0 reduce_sum.55
  106.8 13.0 %all_gather.20 = f32[32,4096]{1,0:T(8,128)S(1)} all-gather(f32[32,1024]{1,0:T(8,128)S(1)} %add_log_fusion.1), channel_id=1, replica_groups=mesh['traj'=64,'mstate'=4] {'mstate'}, dimensions={1}, use_global_device_ids=true | all-gather | bytes 655360 | tf_op jit(solution)/shard_map/all_gather | solution.py:34
  119.8 209.4 %all-reduce.4.cloned.1.call-done = f32[32,4096]{1,0:T(8,128)} async-done(((f32[32,4096]{1,0:T(8,128)}), f32[32,4096]{1,0:T(8,128)}) %all-reduce.4.cloned.1.call-update) | async-done | bytes 524304 | tf_op jit(solution)/shard_map/psum | solution.py:18
  332.8 27.7 %gather_fusion = f32[8192,32]{1,0:T(8,128)} fusion(f32[32,4096]{0,1:T(8,128)S(1)} %copy.43, s32[8192]{0:T(1024)S(1)} %fusion.12), kind=kCustom, calls=%fused_computation.clone | custom fusion | bytes 2129920 | tf_op jit(solution)/shard_map/jit(_take)/gather | solution.py:36
  360.5 6.5 fusion.8
  367.1 4.0 exponential_reduce_fusion.1
  371.3 75.6 %pmax.14 = f32[32]{0:T(128)S(1)} all-reduce(f32[32]{0:T(128)S(1)} %subtract_reduce_fusion.1), channel_id=1, replica_groups=mesh['traj'=64,'mstate'=4] {'traj','mstate'}, use_global_device_ids=true, to_apply=%region_7.9 | all-reduce | flops 32 | bytes 256 | tf_op jit(solution)/shard_map/pmax | solution.py:40
  449.8 44.8 %scatter_custom_fusion.1 = f32[4096,32]{1,0:T(8,128)S(1)} fusion(s32[8192]{0:T(1024)S(1)} %copy-done.10, f32[8192,32]{1,0:T(8,128)} %copy.45, f32[]{:T(128)} %constant.11.clone.1), kind=kCustom, calls=%fused_computation.19 | custom fusion | flops 262144 | bytes 524800 | tf_op jit(solution)/shard_map/scatter-add | solution.py:42
  498.0 249.8 %all-reduce.6.cloned.1.call-done = f32[32,4096]{1,0:T(8,128)} async-done(((f32[32,4096]{1,0:T(8,128)}), f32[32,4096]{1,0:T(8,128)}) %all-reduce.6.cloned.1.call-update) | async-done | bytes 524304 | tf_op jit(solution)/shard_map/psum | solution.py:43
  749.0 6.7 multiply_reduce_fusion
  755.8 81.9 %all-gather.7.cloned.1.call-done = f32[2048,1024]{1,0:T(8,128)} async-done(((f32[32,1024]{1,0:T(8,128)}), f32[2048,1024]{1,0:T(8,128)}) %all-gather.7.cloned.1.call-update) | async-done | bytes 8388624 | tf_op jit(solution)/shard_map/all_gather | solution.py:33
  837.7 4.0 reduce_sum.58
  841.7 13.4 %all_gather.23 = f32[32,4096]{1,0:T(8,128)S(1)} all-gather(f32[32,1024]{1,0:T(8,128)S(1)} %add_log_fusion), channel_id=1, replica_groups=mesh['traj'=64,'mstate'=4] {'mstate'}, dimensions={1}, use_global_device_ids=true | all-gather | bytes 655360 | tf_op jit(solution)/shard_map/all_gather | solution.py:34
  858.6 27.7 %gather_fusion.1 = f32[8192,32]{1,0:T(8,128)} fusion(f32[32,4096]{0,1:T(8,128)S(1)} %copy.47, s32[8192]{0:T(1024)S(1)} %fusion.12), kind=kCustom, calls=%fused_computation.1.clone | custom fusion | bytes 2129920 | tf_op jit(solution)/shard_map/jit(_take)/gather | solution.py:36
  886.3 6.5 fusion.9
  892.8 4.0 exponential_reduce_fusion
  897.1 72.3 %pmax.15 = f32[32]{0:T(128)S(1)} all-reduce(f32[32]{0:T(128)S(1)} %subtract_reduce_fusion), channel_id=1, replica_groups=mesh['traj'=64,'mstate'=4] {'traj','mstate'}, use_global_device_ids=true, to_apply=%region_15.17 | all-reduce | flops 32 | bytes 256 | tf_op jit(solution)/shard_map/pmax | solution.py:40
  969.6 2.6 copy.49
  972.2 45.7 %scatter_custom_fusion.2 = f32[4096,32]{1,0:T(8,128)} fusion(s32[8192]{0:T(1024)S(1)} %copy-done.10, f32[8192,32]{1,0:T(8,128)} %copy.49, f32[]{:T(128)} %constant.11.clone.1), kind=kCustom, calls=%fused_computation.17 | custom fusion | flops 262144 | bytes 524800 | tf_op jit(solution)/shard_map/scatter-add | solution.py:42
  1019.5 259.3 %all-reduce.8.cloned.1.call-done = f32[32,4096]{0,1:T(8,128)} async-done(((f32[32,4096]{0,1:T(8,128)}), f32[32,4096]{0,1:T(8,128)}) %all-reduce.8.cloned.1.call-update) | async-done | bytes 524304 | tf_op jit(solution)/shard_map/psum | solution.py:43
  (61 shorter events, 22.4 us)
Async XLA Ops:
  8.0 94.8 %all-gather.5.cloned.1.call-start = ((), (), s32[]{:S(2)}) async-start(), calls=%async_computation.3 | async-start | bytes 8519680 | tf_op jit(solution)/shard_map/all_gather | solution.py:33
  9.9 6.7 copy-start.10
  9.9 6.7 copy-start.11
  16.5 50.3 %copy-start.2 = (f32[32,8192]{1,0:T(8,128)S(1)}, f32[32,8192]{1,0:T(8,128)}, u32[]{:S(2)}) copy-start(f32[32,8192]{1,0:T(8,128)} %param.8) | copy-start | bytes 3145732
  16.5 312.6 %all-reduce.4.cloned.1.call-start = ((), (), s32[]{:S(2)}) async-start(), calls=%async_computation | async-start | bytes 1048576 | tf_op jit(solution)/shard_map/psum | solution.py:18
  66.7 681.1 %all-reduce.6.cloned.1.call-start = ((), (), s32[]{:S(2)}) async-start(), calls=%async_computation.1 | async-start | bytes 1048576 | tf_op jit(solution)/shard_map/psum | solution.py:43
  102.8 226.4 %copy-start.9 = (f32[32,4096]{1,0:T(8,128)S(1)}, f32[32,4096]{1,0:T(8,128)}, u32[]{:S(2)}) copy-start(f32[32,4096]{1,0:T(8,128)} %param.12) | copy-start | bytes 1572868
  119.8 209.4 %copy-start.5 = (f32[32,4096]{1,0:T(8,128)}, f32[32,4096]{1,0:T(8,128)S(1)}, u32[]{:S(2)}) copy-start(f32[32,4096]{1,0:T(8,128)S(1)} %all_gather.20) | copy-start | bytes 1572868
  360.5 6.5 copy-start
  360.5 6.5 copy-start.4
  496.0 341.6 %all-gather.7.cloned.1.call-start = ((), (), s32[]{:S(2)}) async-start(), calls=%async_computation.4 | async-start | bytes 8519680 | tf_op jit(solution)/shard_map/all_gather | solution.py:33
  755.7 523.1 %all-reduce.8.cloned.1.call-start = ((), (), s32[]{:S(2)}) async-start(), calls=%async_computation.2 | async-start | bytes 4194304 | tf_op jit(solution)/shard_map/psum | solution.py:43
  837.7 18.2 %copy-start.7 = (f32[32,4096]{1,0:T(8,128)S(1)}, f32[32,4096]{1,0:T(8,128)}, u32[]{:S(2)}) copy-start(f32[32,4096]{1,0:T(8,128)} %all-reduce.6.cloned.1.call-done) | copy-start | bytes 1572868
  837.7 18.2 %copy-start.8 = (f32[32,4096]{1,0:T(8,128)S(1)}, f32[32,4096]{1,0:T(8,128)}, u32[]{:S(2)}) copy-start(f32[32,4096]{1,0:T(8,128)} %all-reduce.4.cloned.1.call-done) | copy-start | bytes 1572868
  855.1 0.8 copy-start.6
  886.3 6.5 copy-start.1
  886.3 6.5 copy-start.3
Sparse Core Ops, SparseCore 0:
  16.6 86.0 all-gather.4
  755.8 81.8 all-gather.6
Sparse Core Ops, SparseCore 1:
  66.8 262.3 all-reduce.3
  496.1 251.6 all-reduce.5
  1018.0 260.7 all-reduce.7
